TPU v7x, 32 devices: a whole 2x2x4 slice. The times are simulated.
32 devices in a mesh: seq: 8 (over z, y), fsdp: 4 (over x, core).
Axes of the slice: x: 2, y: 2, z: 4, core: 2. Of those that a mesh axis runs over, the one named last changes fastest.
Arguments:
- tokens: bfloat16 [2048, 2048], P('seq', 'fsdp'), may hold values from -6 to 6
- deal_order: int32 [8, 8], replicated, may hold values from 0 to 7, each once within a row
- lengths: int32 [4], replicated, may hold values from 1 to 1024, 2048 in all
- x_weight: bfloat16 [2048, 1536], P(None, 'fsdp'), may hold values from -0.0390625 to 0.0390625
- z_weight: bfloat16 [2048, 1536], P(None, 'fsdp'), may hold values from -0.125 to 0.125
- shared_weight: bfloat16 [2048, 512], P('fsdp'), may hold values from -0.0390625 to 0.0390625
- step_weight: bfloat16 [2048, 24], P(None, 'fsdp'), may hold values from -0.125 to 0.125
- conv_heads: float32 [4, 1536], P(None, 'fsdp'), may hold values from -3 to 3
- conv_shared: float32 [4, 512], replicated, may hold values from -3 to 3
- step_bias: float32 [24], P('fsdp'), as said below
- decay_log: float32 [24], P('fsdp'), may hold values from -7.1 to -2.8, as said below
- skip_gain: float32 [24], P('fsdp'), may hold values from 0.5 to 1.5
Outputs:
- mixed: bfloat16 [2048, 1536], P('seq', 'fsdp')
Inputs may be any that keep to these rules, and one draw needn't show every extreme that they name: `deal_order`: each row is a permutation of 0 to 7. The lengths sum to 2048. `decay_log`: one value a head. `step_bias`: one value a head.
All inputs are finite; a program needn't handle non-finite values.
Results may differ from a plain program's by a relative error of at most 0.0095.
Values may be sent and summed in bfloat16 or wider, within the bound.
No kernel may reach another device: no remote copies, remote signals or barrier semaphores. Data moves between devices by JAX's collectives and lax.ppermute only.
A program may use at most 128 MiB of HBM per device.

v0:
```python
import jax
import jax.numpy as jnp
from jax import lax
from jax.sharding import PartitionSpec as P

precise = lax.Precision.HIGHEST


def shifted(array, axis, by):
    count = lax.axis_size(axis)
    pairs = [(i, i + by) for i in range(count) if 0 <= i + by < count]
    return lax.ppermute(array, axis, pairs)


def prefix(part, axis, combine, identity):
    place = lax.axis_index(axis)
    gathered = jax.tree.map(lambda a: lax.all_gather(a, axis), part)
    state = jax.tree.map(lambda a, e: jnp.zeros_like(a) + jnp.asarray(e, a.dtype), part, identity)

    def one(turn, state):
        return combine(
            state, jax.tree.map(lambda a: lax.dynamic_index_in_dim(a, turn, 0, False), gathered)
        )

    return lax.fori_loop(0, place, one, state)


def segment_of(positions, lengths):
    prompt_ends = jnp.cumsum(lengths)
    counted = (positions[:, None] >= prompt_ends[None, :]).astype(jnp.int32)
    return jnp.sum(counted, axis=1)


def causal_conv(extended, segment_ids, weights, conv_width):
    out_rows = extended.shape[0] - conv_width + 1
    target = segment_ids[conv_width - 1 :]
    running = jnp.zeros((out_rows, extended.shape[1]), jnp.float32)
    for tap_index in range(conv_width):
        matched = (segment_ids[tap_index : tap_index + out_rows] == target).astype(jnp.float32)
        running = (
            running
            + weights[tap_index][None, :]
            * extended[tap_index : tap_index + out_rows]
            * matched[:, None]
        )
    return running


def local_terms(x_heads, b_rows, c_rows, step_size, decay_log, segment_ids, seg_before):
    log_decay = -jnp.exp(decay_log)[None, :] * step_size
    cum_decay = jnp.cumsum(log_decay, axis=0)
    positions_in = jnp.arange(x_heads.shape[0], dtype=jnp.int32)
    same_prompt = (segment_ids[:, None] == segment_ids[None, :]) & (
        positions_in[:, None] >= positions_in[None, :]
    )
    decay_gap = cum_decay.T[:, :, None] - cum_decay.T[:, None, :]
    decay_matrix = jnp.exp(jnp.where(same_prompt[None], decay_gap, -jnp.inf))
    scores = jnp.dot(c_rows, b_rows.T, precision=precise)
    x_step = x_heads * step_size[:, :, None]
    intra = jnp.einsum("hts,shp->thp", scores[None] * decay_matrix, x_step, precision=precise)
    to_end = jnp.exp(
        jnp.where(
            (segment_ids == segment_ids[-1])[:, None], cum_decay[-1][None, :] - cum_decay, -jnp.inf
        )
    )
    state_out = jnp.einsum("shp,sn->hpn", x_step * to_end[:, :, None], b_rows, precision=precise)
    carried = segment_ids == seg_before
    carry_in = jnp.exp(jnp.where(carried[:, None], cum_decay, -jnp.inf))
    block_decay = jnp.where(carried[-1], jnp.exp(cum_decay[-1]), 0.0)
    return (intra, state_out, carry_in, block_decay)


def combine(earlier, later):
    return (earlier[0] * later[0], later[0][:, None, None] * earlier[1] + later[1])


def per_device(
    tokens,
    deal_order,
    lengths,
    x_weight,
    z_weight,
    shared_weight,
    step_weight,
    conv_heads,
    conv_shared,
    step_bias,
    decay_log,
    skip_gain,
):
    seq_count = lax.axis_size("seq")
    own_index = lax.axis_index("seq")
    tok_dev = tokens.shape[0]
    piece_rows = tok_dev // seq_count
    slot_rows = tokens.reshape(seq_count, piece_rows, tokens.shape[1])
    arrived = lax.all_to_all(slot_rows, "seq", split_axis=0, concat_axis=0, tiled=True)
    dealt_row = lax.dynamic_slice_in_dim(deal_order, own_index, 1, 0)[0]
    inverse = jnp.argsort(dealt_row)
    stream_block = jnp.take(arrived, inverse, axis=0).reshape(tok_dev, tokens.shape[1])
    inner_dev = x_weight.shape[1]
    heads_dev = step_weight.shape[1]
    head_dim = inner_dev // heads_dev
    state_dim = shared_weight.shape[1] // 2
    w_full = lax.all_gather(shared_weight, "fsdp", axis=0, tiled=True)
    weight_list = (x_weight, z_weight, step_weight, w_full)
    feature_part = lax.all_gather(stream_block, "fsdp", axis=1, tiled=True)
    x_acc, z_acc, step_acc, bc_acc = tuple(
        (
            jnp.dot(feature_part, weight, preferred_element_type=jnp.float32)
            for weight in weight_list
        )
    )
    x_raw = x_acc.astype(jnp.bfloat16)
    z_raw = z_acc.astype(jnp.bfloat16)
    bc_raw = bc_acc.astype(jnp.bfloat16)
    step_size = jax.nn.softplus(step_acc + step_bias[None, :])
    mixed_in = jnp.concatenate([x_raw, bc_raw], axis=1)
    conv_width = conv_heads.shape[0]
    prior_rows = shifted(mixed_in[tok_dev - conv_width + 1 :], "seq", 1)
    first_pos = own_index * tok_dev
    positions = first_pos - (conv_width - 1) + jnp.arange(tok_dev + conv_width - 1, dtype=jnp.int32)
    seg_ext = segment_of(positions, lengths)
    extended = jnp.concatenate([prior_rows, mixed_in], axis=0).astype(jnp.float32)
    activated = jax.nn.silu(
        causal_conv(
            extended, seg_ext, jnp.concatenate([conv_heads, conv_shared], axis=1), conv_width
        )
    )
    segment_ids = seg_ext[conv_width - 1 :]
    seg_before = jnp.where(own_index == 0, -1, seg_ext[conv_width - 2])
    x_heads = activated[:, :inner_dev].reshape(tok_dev, heads_dev, head_dim)
    b_rows = activated[:, inner_dev : inner_dev + state_dim]
    c_rows = activated[:, inner_dev + state_dim :]
    intra, state_out, carry_in, block_decay = local_terms(
        x_heads, b_rows, c_rows, step_size, decay_log, segment_ids, seg_before
    )
    identity = (jnp.ones_like(block_decay), jnp.zeros_like(state_out))
    _, state_in = prefix((block_decay, state_out), "seq", combine, identity)
    incoming = jnp.einsum("tn,hpn->thp", c_rows, state_in, precision=precise)
    y_block = intra + carry_in[:, :, None] * incoming + skip_gain[None, :, None] * x_heads
    gated = (y_block.reshape(tok_dev, inner_dev) * jax.nn.silu(z_raw.astype(jnp.float32))).astype(
        jnp.bfloat16
    )
    ordered = gated.reshape(seq_count, piece_rows, inner_dev)
    outgoing = jnp.take(ordered, dealt_row, axis=0)
    returned = lax.all_to_all(outgoing, "seq", split_axis=0, concat_axis=0, tiled=True)
    return returned.reshape(tok_dev, inner_dev)


def solution(mesh):
    return jax.shard_map(
        per_device,
        mesh=mesh,
        in_specs=(
            P("seq", "fsdp"),
            P(),
            P(),
            P(None, "fsdp"),
            P(None, "fsdp"),
            P("fsdp", None),
            P(None, "fsdp"),
            P(None, "fsdp"),
            P(),
            P("fsdp"),
            P("fsdp"),
            P("fsdp"),
        ),
        out_specs=P("seq", "fsdp"),
        check_vma=False,
    )
```

profile of v0, /device:TPU:0, one launch (start us, length us, event | category | flops | bytes accessed | tf_op | source)
XLA Modules:
  0.0 173.2 jit_solution(6664324433288918847)
XLA Ops:
  6.6 7.4 %all-to-all-start = ((bf16[8,32,512]{2,1,0:T(8,128)(2,1)}), bf16[8,32,512]{2,1,0:T(8,128)(2,1)S(1)}, u32[]{:S(2)}, u32[]{:S(2)}) async-start(bf16[8,32,512]{2,1,0:T(8,128)(2,1)} %bitcast.90), calls=%async_computation | async-start | bytes 524288 | tf_op jit(solution)/shard_map/all_to_all | solution.py:96
  14.0 1.3 compare_and_fusion.1
  15.3 1.0 sort.17
  16.5 6.5 %all-to-all-done = bf16[8,32,512]{2,1,0:T(8,128)(2,1)S(1)} async-done(((bf16[8,32,512]{2,1,0:T(8,128)(2,1)}), bf16[8,32,512]{2,1,0:T(8,128)(2,1)S(1)}, u32[]{:S(2)}, u32[]{:S(2)}) %all-to-all-start) | async-done | bytes 262176 | tf_op jit(solution)/shard_map/all_to_all | solution.py:96
  22.9 0.6 gather_fusion
  23.5 0.8 bitcast_select_fusion
  24.4 0.7 all-gather.8.cloned.1.call-update
  25.4 0.6 fusion.51
  26.6 0.7 broadcast_compare_fusion
  27.4 0.6 slice.89
  28.0 12.2 %all-gather.6.cloned.1.call-done = bf16[256,2048]{1,0:T(8,128)(2,1)} async-done(((bf16[256,512]{1,0:T(8,128)(2,1)}), bf16[256,2048]{1,0:T(8,128)(2,1)}) %all-gather.6.cloned.1.call-update) | async-done | bytes 1048592 | tf_op jit(solution)/shard_map/all_gather | solution.py:106
  40.3 1.6 fusion.41
  41.9 1.8 %reduce-window.19 = f32[6,2,128]{2,1,0:T(2,128)S(1)} reduce-window(f32[6,2,128]{2,1,0:T(2,128)S(1)} %reshape.175, f32[]{:T(128)} %constant.76.clone.1), window={size=1x1x128 pad=0_0x0_0x127_0}, to_apply=%region_3.4 | reduce-window | flops 195072 | bytes 12292 | tf_op jit(solution)/shard_map/reduce-window.1
  44.2 0.8 slice_reduce_fusion
  45.1 1.9 %convolution_convert_fusion.2 = bf16[256,384]{1,0:T(8,128)(2,1)S(1)} fusion(bf16[256,2048]{1,0:T(8,128)(2,1)} %all-gather.6.cloned.1.call-done, bf16[2048,384]{1,0:T(8,128)(2,1)S(1)} %copy-done), kind=kOutput, calls=%fused_computation.16 | convolution fusion | flops 402751488 | bytes 2818048 | tf_op jit(solution)/shard_map/dot_general | solution.py:109
  47.0 17.4 %all-gather.8.cloned.1.call-done = bf16[2048,512]{1,0:T(8,128)(2,1)} async-done(((bf16[512,512]{1,0:T(8,128)(2,1)}), bf16[2048,512]{1,0:T(8,128)(2,1)}) %all-gather.8.cloned.1.call-update) | async-done | bytes 2097168 | tf_op jit(solution)/shard_map/all_gather | solution.py:104
  64.5 2.3 %convolution_convert_fusion = bf16[256,512]{1,0:T(8,128)(2,1)S(1)} fusion(bf16[256,2048]{1,0:T(8,128)(2,1)S(1)} %copy-done.1, bf16[2048,512]{1,0:T(8,128)(2,1)} %all-gather.8.cloned.1.call-done), kind=kOutput, calls=%fused_computation.12 | convolution fusion | flops 537001984 | bytes 3407872 | tf_op jit(solution)/shard_map/dot_general | solution.py:109
  66.8 3.4 %collective-permute-start = (bf16[3,896]{1,0:T(4,128)(2,1)S(1)}, bf16[3,896]{1,0:T(4,128)(2,1)S(1)}, u32[]{:S(2)}, u32[]{:S(2)}) collective-permute-start(bf16[3,896]{1,0:T(4,128)(2,1)S(1)} %pad_maximum_fusion), channel_id=1, source_target_pairs={{0,4},{4,8},{8,12},{12,16},{16,20},{20,24},{24,28},{1,5},{5,9},{9,... | collective-permute-start | bytes 16136 | tf_op jit(solution)/shard_map/ppermute | solution.py:12
  70.2 1.3 collective-permute-done
  71.6 0.7 divide_multiply_fusion
  72.5 1.2 fusion.26
  73.8 0.7 fusion.47
  74.5 0.6 pad_clamp_fusion
  75.1 0.7 fusion.32
  75.9 21.6 %all-gather.1 = f32[8,1,6]{2,1,0:T(1,128)} all-gather(f32[1,1,6]{2,1,0:T(1,128)S(1)} %bitcast.96), channel_id=1, replica_groups=mesh['seq'=8,'fsdp'=4] {'seq'}, dimensions={0}, use_global_device_ids=true | all-gather | bytes 216 | tf_op jit(solution)/shard_map/all_gather | solution.py:17
  97.9 37.2 %all-gather.10.cloned.1.call-done = f32[48,64,256]{2,1,0:T(8,128)} async-done(((f32[6,64,256]{2,1,0:T(8,128)}), f32[48,64,256]{2,1,0:T(8,128)}) %all-gather.10.cloned.1.call-update) | async-done | bytes 3145744 | tf_op jit(solution)/shard_map/all_gather | solution.py:17
  135.2 0.5 convolution_multiply_fusion
  135.7 2.8 %fusion.11 = f32[256,6,64]{0,2,1:T(8,128)S(1)} fusion(f32[256,6,64]{0,2,1:T(8,128)S(1)} %convolution_multiply_fusion, f32[6,256]{1,0:T(8,128)} %bitcast.93, f32[256,256]{1,0:T(8,128)S(1)} %fusion.34, pred[256,256]{1,0:T(8,128)(4,1)} %fusion.32, f32[256,6,64]{0,2,1:T(8,128)S(1)} %bitcast.86, f32[6]{0:T(128)} %param.25, f32[256,6]{0,1:T(8,128)S(1)} %compare_select_fusion.1), kind=kOutput, calls=%fused_computation.11 | convolution fusion | flops 303562752 | bytes 1519640 | tf_op jit(solution)/shard_map/hts,shp->thp/dot_general | solution.py:60
  138.7 2.5 %multiply_convert_fusion = bf16[256,384]{1,0:T(8,128)(2,1)S(1)} fusion(f32[256,384]{1,0:T(8,128)S(1)} %copy.49, bf16[256,2048]{1,0:T(8,128)(2,1)} %all-gather.6.cloned.1.call-done, bf16[2048,384]{1,0:T(8,128)(2,1)} %param.18), kind=kOutput, calls=%fused_computation.35 | convolution fusion | flops 403439616 | bytes 3211264 | tf_op jit(solution)/shard_map/dot_general | solution.py:109
  141.2 0.7 gather_fusion.1
  142.0 24.0 %all_to_all.10 = bf16[8,32,384]{2,1,0:T(8,128)(2,1)S(1)} all-to-all(bf16[8,32,384]{2,1,0:T(8,128)(2,1)S(1)} %broadcast_select_fusion), channel_id=1, replica_groups=mesh['seq'=8,'fsdp'=4] {'seq'}, dimensions={0} | all-to-all | bytes 393216 | tf_op jit(solution)/shard_map/all_to_all | solution.py:146
  166.0 0.7 copy.67
  (58 shorter events, 2.3 us)
Async XLA Ops:
  6.5 38.6 %copy-start = (bf16[2048,384]{1,0:T(8,128)(2,1)S(1)}, bf16[2048,384]{1,0:T(8,128)(2,1)}, u32[]{:S(2)}) copy-start(bf16[2048,384]{1,0:T(8,128)(2,1)} %param.17) | copy-start | bytes 4718596
  6.5 18.6 %copy-start.8 = (s32[4]{0:T(128)S(1)}, s32[4]{0:T(128)}, u32[]{:S(2)}) copy-start(s32[4]{0:T(128)} %param.16) | copy-start | bytes 52
  6.5 21.4 %copy-start.5 = (f32[4,384]{1,0:T(4,128)S(1)}, f32[4,384]{1,0:T(4,128)}, u32[]{:S(2)}) copy-start(f32[4,384]{1,0:T(4,128)} %param.21) | copy-start | bytes 18436
  6.5 21.4 %copy-start.4 = (f32[4,512]{1,0:T(4,128)S(1)}, f32[4,512]{1,0:T(4,128)}, u32[]{:S(2)}) copy-start(f32[4,512]{1,0:T(4,128)} %param.22) | copy-start | bytes 24580
  6.5 21.5 %copy-start.9 = (f32[6]{0:T(128)S(1)}, f32[6]{0:T(128)}, u32[]{:S(2)}) copy-start(f32[6]{0:T(128)} %param.24) | copy-start | bytes 76
  6.5 33.7 %copy-start.2 = (bf16[2048,6]{0,1:T(8,128)(2,1)S(1)}, bf16[2048,6]{0,1:T(8,128)(2,1)}, u32[]{:S(2)}) copy-start(bf16[2048,6]{0,1:T(8,128)(2,1)} %param.20) | copy-start | bytes 73732
  6.6 33.7 %copy-start.7 = (f32[6]{0:T(128)S(1)}, f32[6]{0:T(128)}, u32[]{:S(2)}) copy-start(f32[6]{0:T(128)} %param.23) | copy-start | bytes 76
  6.6 16.3 %all-to-all-start = ((bf16[8,32,512]{2,1,0:T(8,128)(2,1)}), bf16[8,32,512]{2,1,0:T(8,128)(2,1)S(1)}, u32[]{:S(2)}, u32[]{:S(2)}) async-start(bf16[8,32,512]{2,1,0:T(8,128)(2,1)} %bitcast.90), calls=%async_computation | async-start | bytes 524288 | tf_op jit(solution)/shard_map/all_to_all | solution.py:96
  14.0 26.3 %all-gather.6.cloned.1.call-start = ((), (), s32[]{:S(2)}) async-start(), calls=%async_computation.2 | async-start | bytes 1310720 | tf_op jit(solution)/shard_map/all_gather | solution.py:106
  24.3 40.1 %all-gather.8.cloned.1.call-start = ((), (), s32[]{:S(2)}) async-start(), calls=%async_computation.3 | async-start | bytes 2621440 | tf_op jit(solution)/shard_map/all_gather | solution.py:104
  25.1 110.1 %all-gather.10.cloned.1.call-start = ((), (), s32[]{:S(2)}) async-start(), calls=%async_computation.4 | async-start | bytes 3538944 | tf_op jit(solution)/shard_map/all_gather | solution.py:17
  41.9 22.5 %copy-start.1 = (bf16[256,2048]{1,0:T(8,128)(2,1)S(1)}, bf16[256,2048]{1,0:T(8,128)(2,1)}, u32[]{:S(2)}) copy-start(bf16[256,2048]{1,0:T(8,128)(2,1)} %all-gather.6.cloned.1.call-done) | copy-start | bytes 3145732
  44.2 0.8 copy-start.3
  66.8 4.7 %collective-permute-start = (bf16[3,896]{1,0:T(4,128)(2,1)S(1)}, bf16[3,896]{1,0:T(4,128)(2,1)S(1)}, u32[]{:S(2)}, u32[]{:S(2)}) collective-permute-start(bf16[3,896]{1,0:T(4,128)(2,1)S(1)} %pad_maximum_fusion), channel_id=1, source_target_pairs={{0,4},{4,8},{8,12},{12,16},{16,20},{20,24},{24,28},{1,5},{5,9},{9,... | collective-permute-start | bytes 16136 | tf_op jit(solution)/shard_map/ppermute | solution.py:12
  138.7 3.2 %copy-start.6 = (pred[8]{0:T(512)(128)(4,1)S(1)}, pred[8]{0:T(512)(128)(4,1)}, u32[]{:S(2)}) copy-start(pred[8]{0:T(512)(128)(4,1)} %get-tuple-element.68) | copy-start | bytes 28
Sparse Core Ops, SparseCore 0:
  24.5 15.7 all-gather.5
  41.8 22.5 all-gather.7
  73.9 61.2 all-gather.9
where the time goes:
time: 174 us; the launch traced here: 173 us
  waiting for transfers between devices  75.4 us (43%)
  blocking collectives  45.7 us (26%)
  between operations  14 us (8%)
  matrix products  13.3 us (8%)
  starting transfers between devices  10.9 us (6%)
  other arithmetic  9.84 us (6%)
  local copies, waits for them, and re-layouts  4.14 us (2%)
    all_gather x1, waiting for transfers between devices, prefix(): gathered = jax.tree.map(lambda a: lax.all_gather(a, axis), part)  37.2 us
    all_to_all x1, blocking collectives, per_device(): lax.all_to_all(outgoing, 'seq', split_axis=0, concat_axis=0, tiled=True)  24 us
    all_gather x1, blocking collectives, prefix(): gathered = jax.tree.map(lambda a: lax.all_gather(a, axis), part)  21.6 us
    all_gather x1, waiting for transfers between devices, per_device(): w_full = lax.all_gather(shared_weight, 'fsdp', axis=0, tiled=True)  17.4 us
    all_gather x1, waiting for transfers between devices, per_device(): feature_part = lax.all_gather(stream_block, 'fsdp', axis=1, tiled=True)  12.2 us
    dot_general x4, matrix products, per_device(): jnp.dot(feature_part, weight, preferred_element_type=jnp.float32)  8.34 us
    all_to_all x1, starting transfers between devices, per_device(): lax.all_to_all(slot_rows, 'seq', split_axis=0, concat_axis=0, tiled=True)  7.42 us
    all_to_all x1, waiting for transfers between devices, per_device(): lax.all_to_all(slot_rows, 'seq', split_axis=0, concat_axis=0, tiled=True)  6.45 us
  transfers between devices with their start and end apart: 5, of which 5 were waited for; matrix products, arithmetic and copies ran while one was open for 8% of the time, Pallas kernels for 0%

commit v1 on v0

--- a/solution.py
+++ b/solution.py
@@ -4,6 +4,29 @@
 from jax.sharding import PartitionSpec as P
 
 precise = lax.Precision.HIGHEST
+
+
+def in_blocks(value, dim, count):
+    dims = value.shape
+    parts = value.reshape(*dims[:dim], count, dims[dim] // count, *dims[dim + 1 :])
+    return jnp.moveaxis(parts, dim, 0)
+
+
+def joined_along(pieces, dim):
+    pieces = jnp.moveaxis(pieces, 0, dim)
+    dims = pieces.shape
+    return pieces.reshape(*dims[:dim], dims[dim] * dims[dim + 1], *dims[dim + 2 :])
+
+
+def pairwise_exchange(x, axis, split_dim, concat_dim):
+    count, index = (lax.axis_size(axis), lax.axis_index(axis))
+    blocks = in_blocks(x, split_dim, count)
+    outs = [blocks[index]]
+    for step in range(1, count):
+        sent = blocks[index ^ step]
+        outs.append(lax.ppermute(sent, axis, [(i, i ^ step) for i in range(count)]))
+    blocks = jnp.stack(outs)[index ^ jnp.arange(count)]
+    return joined_along(blocks, concat_dim)
 
 
 def shifted(array, axis, by):
@@ -143,7 +166,7 @@
     )
     ordered = gated.reshape(seq_count, piece_rows, inner_dev)
     outgoing = jnp.take(ordered, dealt_row, axis=0)
-    returned = lax.all_to_all(outgoing, "seq", split_axis=0, concat_axis=0, tiled=True)
+    returned = pairwise_exchange(outgoing, "seq", 0, 0)
     return returned.reshape(tok_dev, inner_dev)
 
 

time: 174 us -> 179 us (1.029)
  blocking collectives: 45.7 us -> 21.8 us
  starting transfers between devices: 10.9 us -> 32.3 us
  waiting for transfers between devices: 75.4 us -> 81.1 us
    all_to_all x1 -> x0, blocking collectives: 24 us -> none  [per_device(): lax.all_to_all(outgoing, 'seq', split_axis=0, concat_axis=0, tiled=True)]
    ppermute x0 -> x7, starting transfers between devices: none -> 21.4 us  [pairwise_exchange(): outs.append(lax.ppermute(sent, axis, [(i, i ^ step) for i in range(count)]))]
    ppermute x0 -> x7, waiting for transfers between devices: none -> 6.43 us  [pairwise_exchange(): outs.append(lax.ppermute(sent, axis, [(i, i ^ step) for i in range(count)]))]
  transfers between devices with their start and end apart: 5 -> 12, of which waited for: 5 -> 8; matrix products, arithmetic and copies ran while one was open for 8% -> 8% of each run, Pallas kernels for 0% -> 0%
where the time goes in v1:
time: 179 us; the launch traced here: 178 us
  waiting for transfers between devices  81.1 us (45%)
  starting transfers between devices  32.3 us (18%)
  blocking collectives  21.8 us (12%)
  between operations  14 us (8%)
  matrix products  13.3 us (7%)
  other arithmetic  10.4 us (6%)
  local copies, waits for them, and re-layouts  4.97 us (3%)
    all_gather x1, waiting for transfers between devices, prefix(): gathered = jax.tree.map(lambda a: lax.all_gather(a, axis), part)  36.5 us
    all_gather x1, blocking collectives, prefix(): gathered = jax.tree.map(lambda a: lax.all_gather(a, axis), part)  21.8 us
    ppermute x7, starting transfers between devices, pairwise_exchange(): outs.append(lax.ppermute(sent, axis, [(i, i ^ step) for i in range(count)]))  21.4 us
    all_gather x1, waiting for transfers between devices, per_device(): w_full = lax.all_gather(shared_weight, 'fsdp', axis=0, tiled=True)  17.4 us
    all_gather x1, waiting for transfers between devices, per_device(): feature_part = lax.all_gather(stream_block, 'fsdp', axis=1, tiled=True)  12.2 us
    dot_general x4, matrix products, per_device(): jnp.dot(feature_part, weight, preferred_element_type=jnp.float32)  8.34 us
    all_to_all x1, starting transfers between devices, per_device(): lax.all_to_all(slot_rows, 'seq', split_axis=0, concat_axis=0, tiled=True)  7.42 us
    all_to_all x1, waiting for transfers between devices, per_device(): lax.all_to_all(slot_rows, 'seq', split_axis=0, concat_axis=0, tiled=True)  6.49 us
  transfers between devices with their start and end apart: 12, of which 8 were waited for; matrix products, arithmetic and copies ran while one was open for 8% of the time, Pallas kernels for 0%

profile of v1, /device:TPU:0, one launch (start us, length us, event | category | flops | bytes accessed | tf_op | source)
XLA Modules:
  0.0 177.9 jit_solution(2266336260900227268)
XLA Ops:
  6.6 7.4 %all-to-all-start = ((bf16[8,32,512]{2,1,0:T(8,128)(2,1)}), bf16[8,32,512]{2,1,0:T(8,128)(2,1)S(1)}, u32[]{:S(2)}, u32[]{:S(2)}) async-start(bf16[8,32,512]{2,1,0:T(8,128)(2,1)} %bitcast.108), calls=%async_computation | async-start | bytes 524288 | tf_op jit(solution)/shard_map/all_to_all | solution.py:119
  14.0 1.2 compare_and_fusion.1
  15.3 1.0 sort.17
  16.4 6.5 %all-to-all-done = bf16[8,32,512]{2,1,0:T(8,128)(2,1)S(1)} async-done(((bf16[8,32,512]{2,1,0:T(8,128)(2,1)}), bf16[8,32,512]{2,1,0:T(8,128)(2,1)S(1)}, u32[]{:S(2)}, u32[]{:S(2)}) %all-to-all-start) | async-done | bytes 262176 | tf_op jit(solution)/shard_map/all_to_all | solution.py:119
  23.5 0.8 bitcast_select_fusion
  24.4 0.7 all-gather.8.cloned.1.call-update
  26.7 0.7 broadcast_compare_fusion
  28.1 12.2 %all-gather.6.cloned.1.call-done = bf16[256,2048]{1,0:T(8,128)(2,1)} async-done(((bf16[256,512]{1,0:T(8,128)(2,1)}), bf16[256,2048]{1,0:T(8,128)(2,1)}) %all-gather.6.cloned.1.call-update) | async-done | bytes 1048592 | tf_op jit(solution)/shard_map/all_gather | solution.py:129
  40.3 1.6 fusion.41
  42.0 1.8 %reduce-window.19 = f32[6,2,128]{2,1,0:T(2,128)S(1)} reduce-window(f32[6,2,128]{2,1,0:T(2,128)S(1)} %reshape.204, f32[]{:T(128)} %constant.84.clone.1), window={size=1x1x128 pad=0_0x0_0x127_0}, to_apply=%region_3.4 | reduce-window | flops 195072 | bytes 12292 | tf_op jit(solution)/shard_map/reduce-window.1
  44.2 0.8 slice_reduce_fusion
  45.1 1.9 %convolution_convert_fusion.2 = bf16[256,384]{1,0:T(8,128)(2,1)S(1)} fusion(bf16[256,2048]{1,0:T(8,128)(2,1)} %all-gather.6.cloned.1.call-done, bf16[2048,384]{1,0:T(8,128)(2,1)S(1)} %copy-done), kind=kOutput, calls=%fused_computation.17 | convolution fusion | flops 402751488 | bytes 2818048 | tf_op jit(solution)/shard_map/dot_general | solution.py:132
  47.1 17.4 %all-gather.8.cloned.1.call-done = bf16[2048,512]{1,0:T(8,128)(2,1)} async-done(((bf16[512,512]{1,0:T(8,128)(2,1)}), bf16[2048,512]{1,0:T(8,128)(2,1)}) %all-gather.8.cloned.1.call-update) | async-done | bytes 2097168 | tf_op jit(solution)/shard_map/all_gather | solution.py:127
  64.5 2.3 %convolution_convert_fusion = bf16[256,512]{1,0:T(8,128)(2,1)S(1)} fusion(bf16[256,2048]{1,0:T(8,128)(2,1)S(1)} %copy-done.1, bf16[2048,512]{1,0:T(8,128)(2,1)} %all-gather.8.cloned.1.call-done), kind=kOutput, calls=%fused_computation.13 | convolution fusion | flops 537001984 | bytes 3407872 | tf_op jit(solution)/shard_map/dot_general | solution.py:132
  66.8 3.4 %collective-permute-start = (bf16[3,896]{1,0:T(4,128)(2,1)S(1)}, bf16[3,896]{1,0:T(4,128)(2,1)S(1)}, u32[]{:S(2)}, u32[]{:S(2)}) collective-permute-start(bf16[3,896]{1,0:T(4,128)(2,1)S(1)} %pad_maximum_fusion), channel_id=1, source_target_pairs={{0,4},{4,8},{8,12},{12,16},{16,20},{20,24},{24,28},{1,5},{5,9},{9,... | collective-permute-start | bytes 16136 | tf_op jit(solution)/shard_map/ppermute | solution.py:35
  70.2 1.3 collective-permute-done
  72.5 1.2 fusion.26
  73.9 0.7 fusion.47
  75.7 0.7 fusion.32
  76.5 21.8 %all-gather.1 = f32[8,1,6]{2,1,0:T(1,128)} all-gather(f32[1,1,6]{2,1,0:T(1,128)S(1)} %bitcast.115), channel_id=1, replica_groups=mesh['seq'=8,'fsdp'=4] {'seq'}, dimensions={0}, use_global_device_ids=true | all-gather | bytes 216 | tf_op jit(solution)/shard_map/all_gather | solution.py:40
  98.7 36.5 %all-gather.10.cloned.1.call-done = f32[48,64,256]{2,1,0:T(8,128)} async-done(((f32[6,64,256]{2,1,0:T(8,128)}), f32[48,64,256]{2,1,0:T(8,128)}) %all-gather.10.cloned.1.call-update) | async-done | bytes 3145744 | tf_op jit(solution)/shard_map/all_gather | solution.py:40
  135.7 2.8 %fusion.11 = f32[256,6,64]{0,2,1:T(8,128)S(1)} fusion(f32[256,6,64]{0,2,1:T(8,128)S(1)} %convolution_multiply_fusion, f32[6,256]{1,0:T(8,128)} %bitcast.112, f32[256,256]{1,0:T(8,128)S(1)} %fusion.34, pred[256,256]{1,0:T(8,128)(4,1)} %fusion.32, f32[256,6,64]{0,2,1:T(8,128)S(1)} %bitcast.105, f32[6]{0:T(128)} %param.25, f32[256,6]{0,1:T(8,128)S(1)} %compare_select_fusion.1), kind=kOutput, calls=%fused_computation.12 | convolution fusion | flops 303562752 | bytes 1519640 | tf_op jit(solution)/shard_map/hts,shp->thp/dot_general | solution.py:83
  138.7 2.5 %multiply_convert_fusion = bf16[256,384]{1,0:T(8,128)(2,1)S(1)} fusion(f32[256,384]{1,0:T(8,128)S(1)} %copy.49, bf16[256,2048]{1,0:T(8,128)(2,1)} %all-gather.6.cloned.1.call-done, bf16[2048,384]{1,0:T(8,128)(2,1)} %param.18), kind=kOutput, calls=%fused_computation.36 | convolution fusion | flops 403439616 | bytes 3211264 | tf_op jit(solution)/shard_map/dot_general | solution.py:132
  141.2 0.7 gather_fusion.1
  142.0 2.5 %collective-permute-start.1 = (bf16[1,32,384]{2,1,0:T(8,128)(2,1)S(1)}, bf16[1,32,384]{2,1,0:T(8,128)(2,1)S(1)}, u32[]{:S(2)}, u32[]{:S(2)}) collective-permute-start(bf16[1,32,384]{2,1,0:T(8,128)(2,1)S(1)} %get-tuple-element.76), channel_id=1, source_target_pairs={{0,4},{4,0},{8,12},{12,8},{16,20},{20,16},{24,28},{28,24},{1,5},{5... | collective-permute-start | bytes 73736 | tf_op jit(solution)/shard_map/ppermute | solution.py:27
  144.5 5.1 %collective-permute-start.2 = (bf16[1,32,384]{2,1,0:T(8,128)(2,1)S(1)}, bf16[1,32,384]{2,1,0:T(8,128)(2,1)S(1)}, u32[]{:S(2)}, u32[]{:S(2)}) collective-permute-start(bf16[1,32,384]{2,1,0:T(8,128)(2,1)S(1)} %get-tuple-element.75), channel_id=1, source_target_pairs={{0,8},{4,12},{8,0},{12,4},{16,24},{20,28},{24,16},{28,20},{1,9},{5... | collective-permute-start | bytes 73736 | tf_op jit(solution)/shard_map/ppermute | solution.py:27
  149.6 8.5 %collective-permute-start.4 = (bf16[1,32,384]{2,1,0:T(8,128)(2,1)S(1)}, bf16[1,32,384]{2,1,0:T(8,128)(2,1)S(1)}, u32[]{:S(2)}, u32[]{:S(2)}) collective-permute-start(bf16[1,32,384]{2,1,0:T(8,128)(2,1)S(1)} %get-tuple-element.73), channel_id=1, source_target_pairs={{0,16},{4,20},{8,24},{12,28},{16,0},{20,4},{24,8},{28,12},{1,17},{... | collective-permute-start | bytes 73736 | tf_op jit(solution)/shard_map/ppermute | solution.py:27
  158.1 0.9 collective-permute-start.5
  159.0 4.4 %collective-permute-start.6 = (bf16[1,32,384]{2,1,0:T(8,128)(2,1)S(1)}, bf16[1,32,384]{2,1,0:T(8,128)(2,1)S(1)}, u32[]{:S(2)}, u32[]{:S(2)}) collective-permute-start(bf16[1,32,384]{2,1,0:T(8,128)(2,1)S(1)} %get-tuple-element.71), channel_id=1, source_target_pairs={{0,24},{4,28},{8,16},{12,20},{16,8},{20,12},{24,0},{28,4},{1,25},{... | collective-permute-start | bytes 73736 | tf_op jit(solution)/shard_map/ppermute | solution.py:27
  163.7 1.7 collective-permute-done.6
  165.5 4.5 %collective-permute-done.7 = bf16[1,32,384]{2,1,0:T(8,128)(2,1)S(1)} collective-permute-done((bf16[1,32,384]{2,1,0:T(8,128)(2,1)S(1)}, bf16[1,32,384]{2,1,0:T(8,128)(2,1)S(1)}, u32[]{:S(2)}, u32[]{:S(2)}) %collective-permute-start.7) | collective-permute-done | bytes 24608 | tf_op jit(solution)/shard_map/ppermute | solution.py:27
  170.0 1.4 gather_fusion.2
  (82 shorter events, 6.8 us)
Async XLA Ops:
  6.5 38.6 %copy-start = (bf16[2048,384]{1,0:T(8,128)(2,1)S(1)}, bf16[2048,384]{1,0:T(8,128)(2,1)}, u32[]{:S(2)}) copy-start(bf16[2048,384]{1,0:T(8,128)(2,1)} %param.17) | copy-start | bytes 4718596
  6.5 18.6 %copy-start.8 = (s32[4]{0:T(128)S(1)}, s32[4]{0:T(128)}, u32[]{:S(2)}) copy-start(s32[4]{0:T(128)} %param.16) | copy-start | bytes 52
  6.5 21.4 %copy-start.5 = (f32[4,384]{1,0:T(4,128)S(1)}, f32[4,384]{1,0:T(4,128)}, u32[]{:S(2)}) copy-start(f32[4,384]{1,0:T(4,128)} %param.21) | copy-start | bytes 18436
  6.5 21.4 %copy-start.4 = (f32[4,512]{1,0:T(4,128)S(1)}, f32[4,512]{1,0:T(4,128)}, u32[]{:S(2)}) copy-start(f32[4,512]{1,0:T(4,128)} %param.22) | copy-start | bytes 24580
  6.5 21.5 %copy-start.9 = (f32[6]{0:T(128)S(1)}, f32[6]{0:T(128)}, u32[]{:S(2)}) copy-start(f32[6]{0:T(128)} %param.24) | copy-start | bytes 76
  6.5 33.7 %copy-start.2 = (bf16[2048,6]{0,1:T(8,128)(2,1)S(1)}, bf16[2048,6]{0,1:T(8,128)(2,1)}, u32[]{:S(2)}) copy-start(bf16[2048,6]{0,1:T(8,128)(2,1)} %param.20) | copy-start | bytes 73732
  6.6 33.7 %copy-start.7 = (f32[6]{0:T(128)S(1)}, f32[6]{0:T(128)}, u32[]{:S(2)}) copy-start(f32[6]{0:T(128)} %param.23) | copy-start | bytes 76
  6.6 16.3 %all-to-all-start = ((bf16[8,32,512]{2,1,0:T(8,128)(2,1)}), bf16[8,32,512]{2,1,0:T(8,128)(2,1)S(1)}, u32[]{:S(2)}, u32[]{:S(2)}) async-start(bf16[8,32,512]{2,1,0:T(8,128)(2,1)} %bitcast.108), calls=%async_computation | async-start | bytes 524288 | tf_op jit(solution)/shard_map/all_to_all | solution.py:119
  14.0 26.3 %all-gather.6.cloned.1.call-start = ((), (), s32[]{:S(2)}) async-start(), calls=%async_computation.1 | async-start | bytes 1310720 | tf_op jit(solution)/shard_map/all_gather | solution.py:129
  24.4 40.1 %all-gather.8.cloned.1.call-start = ((), (), s32[]{:S(2)}) async-start(), calls=%async_computation.2 | async-start | bytes 2621440 | tf_op jit(solution)/shard_map/all_gather | solution.py:127
  25.1 110.1 %all-gather.10.cloned.1.call-start = ((), (), s32[]{:S(2)}) async-start(), calls=%async_computation.3 | async-start | bytes 3538944 | tf_op jit(solution)/shard_map/all_gather | solution.py:40
  41.9 22.5 %copy-start.1 = (bf16[256,2048]{1,0:T(8,128)(2,1)S(1)}, bf16[256,2048]{1,0:T(8,128)(2,1)}, u32[]{:S(2)}) copy-start(bf16[256,2048]{1,0:T(8,128)(2,1)} %all-gather.6.cloned.1.call-done) | copy-start | bytes 3145732
  44.2 0.8 copy-start.3
  66.8 4.7 %collective-permute-start = (bf16[3,896]{1,0:T(4,128)(2,1)S(1)}, bf16[3,896]{1,0:T(4,128)(2,1)S(1)}, u32[]{:S(2)}, u32[]{:S(2)}) collective-permute-start(bf16[3,896]{1,0:T(4,128)(2,1)S(1)} %pad_maximum_fusion), channel_id=1, source_target_pairs={{0,4},{4,8},{8,12},{12,16},{16,20},{20,24},{24,28},{1,5},{5,9},{9,... | collective-permute-start | bytes 16136 | tf_op jit(solution)/shard_map/ppermute | solution.py:35
  138.7 3.2 %copy-start.6 = (pred[8]{0:T(512)(128)(4,1)S(1)}, pred[8]{0:T(512)(128)(4,1)}, u32[]{:S(2)}) copy-start(pred[8]{0:T(512)(128)(4,1)} %get-tuple-element.68) | copy-start | bytes 28
  142.0 17.0 %collective-permute-start.1 = (bf16[1,32,384]{2,1,0:T(8,128)(2,1)S(1)}, bf16[1,32,384]{2,1,0:T(8,128)(2,1)S(1)}, u32[]{:S(2)}, u32[]{:S(2)}) collective-permute-start(bf16[1,32,384]{2,1,0:T(8,128)(2,1)S(1)} %get-tuple-element.76), channel_id=1, source_target_pairs={{0,4},{4,0},{8,12},{12,8},{16,20},{20,16},{24,28},{28,24},{1,5},{5... | collective-permute-start | bytes 73736 | tf_op jit(solution)/shard_map/ppermute | solution.py:27
  144.5 18.9 %collective-permute-start.2 = (bf16[1,32,384]{2,1,0:T(8,128)(2,1)S(1)}, bf16[1,32,384]{2,1,0:T(8,128)(2,1)S(1)}, u32[]{:S(2)}, u32[]{:S(2)}) collective-permute-start(bf16[1,32,384]{2,1,0:T(8,128)(2,1)S(1)} %get-tuple-element.75), channel_id=1, source_target_pairs={{0,8},{4,12},{8,0},{12,4},{16,24},{20,28},{24,16},{28,20},{1,9},{5... | collective-permute-start | bytes 73736 | tf_op jit(solution)/shard_map/ppermute | solution.py:27
  149.6 13.9 %collective-permute-start.3 = (bf16[1,32,384]{2,1,0:T(8,128)(2,1)S(1)}, bf16[1,32,384]{2,1,0:T(8,128)(2,1)S(1)}, u32[]{:S(2)}, u32[]{:S(2)}) collective-permute-start(bf16[1,32,384]{2,1,0:T(8,128)(2,1)S(1)} %get-tuple-element.74), channel_id=1, source_target_pairs={{0,12},{4,8},{8,4},{12,0},{16,28},{20,24},{24,20},{28,16},{1,13},{... | collective-permute-start | bytes 73736 | tf_op jit(solution)/shard_map/ppermute | solution.py:27
  149.6 13.9 %collective-permute-start.4 = (bf16[1,32,384]{2,1,0:T(8,128)(2,1)S(1)}, bf16[1,32,384]{2,1,0:T(8,128)(2,1)S(1)}, u32[]{:S(2)}, u32[]{:S(2)}) collective-permute-start(bf16[1,32,384]{2,1,0:T(8,128)(2,1)S(1)} %get-tuple-element.73), channel_id=1, source_target_pairs={{0,16},{4,20},{8,24},{12,28},{16,0},{20,4},{24,8},{28,12},{1,17},{... | collective-permute-start | bytes 73736 | tf_op jit(solution)/shard_map/ppermute | solution.py:27
  158.1 5.6 %collective-permute-start.5 = (bf16[1,32,384]{2,1,0:T(8,128)(2,1)S(1)}, bf16[1,32,384]{2,1,0:T(8,128)(2,1)S(1)}, u32[]{:S(2)}, u32[]{:S(2)}) collective-permute-start(bf16[1,32,384]{2,1,0:T(8,128)(2,1)S(1)} %get-tuple-element.72), channel_id=1, source_target_pairs={{0,20},{4,16},{8,28},{12,24},{16,4},{20,0},{24,12},{28,8},{1,21},{... | collective-permute-start | bytes 73736 | tf_op jit(solution)/shard_map/ppermute | solution.py:27
  159.0 6.4 %collective-permute-start.6 = (bf16[1,32,384]{2,1,0:T(8,128)(2,1)S(1)}, bf16[1,32,384]{2,1,0:T(8,128)(2,1)S(1)}, u32[]{:S(2)}, u32[]{:S(2)}) collective-permute-start(bf16[1,32,384]{2,1,0:T(8,128)(2,1)S(1)} %get-tuple-element.71), channel_id=1, source_target_pairs={{0,24},{4,28},{8,16},{12,20},{16,8},{20,12},{24,0},{28,4},{1,25},{... | collective-permute-start | bytes 73736 | tf_op jit(solution)/shard_map/ppermute | solution.py:27
  163.4 6.6 %collective-permute-start.7 = (bf16[1,32,384]{2,1,0:T(8,128)(2,1)S(1)}, bf16[1,32,384]{2,1,0:T(8,128)(2,1)S(1)}, u32[]{:S(2)}, u32[]{:S(2)}) collective-permute-start(bf16[1,32,384]{2,1,0:T(8,128)(2,1)S(1)} %get-tuple-element.70), channel_id=1, source_target_pairs={{0,28},{4,24},{8,20},{12,16},{16,12},{20,8},{24,4},{28,0},{1,29},{... | collective-permute-start | bytes 73736 | tf_op jit(solution)/shard_map/ppermute | solution.py:27
Sparse Core Ops, SparseCore 0:
  24.5 15.7 all-gather.5
  41.9 22.5 all-gather.7
  73.9 61.2 all-gather.9
